TPU v7x, 32 devices: a whole 2x2x4 slice. The times are simulated.
32 devices in a mesh: uv: 8 (over y, x, core), chan: 4 (over z).
Axes of the slice: x: 2, y: 2, z: 4, core: 2. Of those that a mesh axis runs over, the one named last changes fastest.
Arguments:
- vis: bfloat16 [98304, 2, 1024], P('uv', None, 'chan'), may hold values from -6 to 6
- row_cell: int32 [98304], P('uv'), may hold values from 0 to 127
- tap_weight: bfloat16 [8, 98304], P(None, 'uv'), may hold values from 0.029907227 to 0.29882812
- tap_offset: int32 [8], replicated, may hold values from -32 to 32
- block_tile: int32 [768], P('uv'), may hold values from 0 to 79, as said below
- tile_owner: int32 [80], replicated, may hold values from 0 to 7, as said below
- galaxy: bfloat16 [152, 128, 2048], P('uv', 'chan'), may hold values from -6 to 6
Outputs:
- delay_cube: bfloat16 [152, 128, 2048], P('uv', 'chan')
- cross_power: float32 [152, 1024], P('uv')
Inputs may be any that keep to these rules, and one draw needn't show every extreme that they name: `tile_owner`: each of the 8 owners holds 1 to 19 tiles, and some owner exactly 19. `block_tile`: of the 96 row blocks of one index of uv, at most 22 lie in tiles of one owner, and exactly 22 lie in the tiles of some owner.
All inputs are finite; a program needn't handle non-finite values.
Results may differ from a plain program's by a relative error of at most 0.0059.
Values may be sent and summed in bfloat16 or wider, within the bound.
No kernel may reach another device: no remote copies, remote signals or barrier semaphores. Data moves between devices by JAX's collectives and lax.ppermute only.
A program may use at most 128 MiB of HBM per device.

v0:
```python
import math
import jax
import jax.numpy as jnp
from jax import lax
from jax.sharding import PartitionSpec as P

CH = 1024
BR = 128
TC = 128
KT = 8


def tile_ranks(tile_owner, owners):
    onehot = (tile_owner[:, None] == jnp.arange(owners, dtype=jnp.int32)[None, :]).astype(jnp.int32)
    before = jnp.cumsum(onehot, axis=0) - onehot
    return jnp.sum(before * onehot, axis=1)


def kernel_matrix(cells, weights, tap_offset):
    positions = jnp.arange(TC, dtype=jnp.int32)
    total = jnp.zeros(cells.shape[:-1] + (TC, cells.shape[-1]), jnp.float32)
    for k in range(KT):
        target = cells + tap_offset[k]
        hit = target[..., None, :] == positions[:, None]
        total = total + jnp.where(
            hit, weights[..., k, :].astype(jnp.float32)[..., None, :], jnp.float32(0.0)
        )
    return total.astype(jnp.bfloat16)


def delay_table():
    freq = jnp.arange(CH, dtype=jnp.int32)
    phase = (freq[:, None] * freq[None, :] % CH).astype(jnp.float32) * jnp.float32(
        2.0 * math.pi / CH
    )
    cosine = jnp.cos(phase)
    sine = jnp.sin(phase)
    x = freq.astype(jnp.float32) * jnp.float32(2.0 * math.pi / CH)
    taper = 0.35875 - 0.48829 * jnp.cos(x) + 0.14128 * jnp.cos(2.0 * x) - 0.01168 * jnp.cos(3.0 * x)
    scale = (taper / jnp.float32(math.sqrt(CH)))[:, None]
    upper = jnp.concatenate([cosine * scale, -sine * scale], axis=1)
    lower = jnp.concatenate([sine * scale, cosine * scale], axis=1)
    return jnp.concatenate([upper, lower], axis=0).astype(jnp.bfloat16)


def _partner_pairs(n, fn):
    return [(i, fn(i)) for i in range(n)]


def _allreduce_sum(x, axis, n):
    if n & n - 1:
        return lax.psum(x, axis)
    d = 1
    while d < n:
        x = x + lax.ppermute(x, axis, _partner_pairs(n, lambda i, d=d: i ^ d))
        d *= 2
    return x


def _gather_pair(part, matrix, pick2, parity, chip, n_owners, slots_dev, after=None):
    pairs = n_owners // 2
    contrib = jnp.einsum("bcr,brf->bcf", matrix, part, preferred_element_type=jnp.float32)
    high = contrib.astype(jnp.bfloat16)
    low = (contrib - high.astype(jnp.float32)).astype(jnp.bfloat16)
    partial = jnp.einsum(
        "sb,bcf->scf",
        pick2,
        jnp.concatenate([high, low], axis=0),
        preferred_element_type=jnp.float32,
    ).astype(jnp.bfloat16)
    partial = partial.reshape((2, pairs, slots_dev) + partial.shape[1:])
    mine = lax.dynamic_index_in_dim(partial, parity, axis=0, keepdims=False)
    other = lax.dynamic_index_in_dim(partial, 1 - parity, axis=0, keepdims=False)
    if after is not None:
        other, _ = lax.optimization_barrier((other, after))
    got = lax.ppermute(other, "uv", _partner_pairs(n_owners, lambda i: i ^ 1))
    pair_send = (mine.astype(jnp.float32) + got.astype(jnp.float32)).astype(jnp.bfloat16)
    own = lax.dynamic_index_in_dim(mine, chip, axis=0, keepdims=False).astype(
        jnp.float32
    ) + lax.dynamic_index_in_dim(got, chip, axis=0, keepdims=False).astype(jnp.float32)
    return (pair_send, own)


def _scatter_pairs(pair_send, own, chip, n_owners):
    pairs = n_owners // 2
    grid = own
    for d in range(1, pairs):
        if pairs & pairs - 1:
            dest = lambda c, d=d: (c + d) % pairs
        else:
            dest = lambda c, d=d: c ^ d
        send = lax.dynamic_index_in_dim(pair_send, dest(chip), axis=0, keepdims=False)
        recv = lax.ppermute(
            send, "uv", _partner_pairs(n_owners, lambda i, dest=dest: dest(i // 2) * 2 + i % 2)
        )
        grid = grid + recv.astype(jnp.float32)
    return grid.astype(jnp.bfloat16)


def body(vis, row_cell, tap_weight, tap_offset, block_tile, tile_owner, galaxy):
    n_owners = lax.axis_size("uv")
    n_chan = lax.axis_size("chan")
    pairs = n_owners // 2
    me = lax.axis_index("uv")
    parity = me % 2
    chip = me // 2
    nblocks = block_tile.shape[0]
    slots_dev = galaxy.shape[0]
    chan_dev = vis.shape[2]
    rank_of_tile = tile_ranks(tile_owner, n_owners)
    owner = tile_owner[block_tile]
    rank = rank_of_tile[block_tile]
    slot = owner % 2 * (pairs * slots_dev) + owner // 2 * slots_dev + rank
    n_slots = n_owners * slots_dev
    pick = (jnp.arange(n_slots, dtype=jnp.int32)[:, None] == slot[None, :]).astype(jnp.bfloat16)
    pick2 = jnp.concatenate([pick, pick], axis=1)
    width = 2 * chan_dev
    blocks = vis.reshape(nblocks, BR, width)
    cells = row_cell.reshape(nblocks, BR)
    weights = jnp.transpose(tap_weight.reshape(KT, nblocks, BR), (1, 0, 2))
    matrix = kernel_matrix(cells, weights, tap_offset)
    table = delay_table()
    cut = width - width // 4
    first = _gather_pair(blocks[:, :, :cut], matrix, pick2, parity, chip, n_owners, slots_dev)
    first_grid = _scatter_pairs(first[0], first[1], chip, n_owners)
    second = _gather_pair(
        blocks[:, :, cut:], matrix, pick2, parity, chip, n_owners, slots_dev, after=first_grid
    )
    table, first_grid = lax.optimization_barrier((table, first_grid))
    second_grid = _scatter_pairs(second[0], second[1], chip, n_owners)
    by_source = table.reshape(2, n_chan, chan_dev, 2 * CH).transpose(1, 0, 2, 3)
    by_source = by_source.reshape(n_chan, width, 2 * CH)
    out = None
    for gridded, lo, hi in ((first_grid, 0, cut), (second_grid, cut, width)):
        piece = lax.all_to_all(gridded, "chan", split_axis=1, concat_axis=2, tiled=True)
        count, cells_part = (piece.shape[0], piece.shape[1])
        rows = by_source[:, lo:hi, :].reshape(n_chan * (hi - lo), 2 * CH)
        term = jnp.dot(
            piece.reshape(count * cells_part, n_chan * (hi - lo)),
            rows,
            preferred_element_type=jnp.float32,
        )
        out = term if out is None else out + term
    delay = out.reshape(count, cells_part, 2 * CH)
    galaxy_f = galaxy.astype(jnp.float32)
    product = delay[..., :CH] * galaxy_f[..., :CH] + delay[..., CH:] * galaxy_f[..., CH:]
    local_power = jnp.sum(product, axis=1)
    power = _allreduce_sum(local_power, "chan", n_chan) / jnp.float32(math.sqrt(TC))
    return (delay.astype(jnp.bfloat16), power)


def solution(mesh):
    return jax.shard_map(
        body,
        mesh=mesh,
        in_specs=(
            P("uv", None, "chan"),
            P("uv"),
            P(None, "uv"),
            P(),
            P("uv"),
            P(),
            P("uv", "chan", None),
        ),
        out_specs=(P("uv", "chan", None), P("uv", None)),
        check_vma=False,
    )
```

profile of v0, /device:TPU:0, one launch (start us, length us, event | category | flops | bytes accessed | tf_op | source)
XLA Modules:
  0.0 397.5 jit_solution(489984688012996538)
XLA Ops:
  4.7 20.5 %reshape.165 = bf16[96,128,512]{2,1,0:T(8,128)(2,1)} reshape(bf16[12288,2,256]{2,1,0:T(2,128)(2,1)} %param.7) | data formatting | bytes 25165824 | tf_op jit(solution)/shard_map/reshape | solution.py:118
  28.2 5.0 %add_bitcast_fusion.10 = (s32[96,128]{1,0:T(8,128)S(1)}, s32[96,128]{1,0:T(8,128)S(1)}, s32[96,128]{1,0:T(8,128)S(1)}, s32[96,128]{1,0:T(8,128)S(1)}, s32[96,128...) fusion(s32[12288]{0:T(1024)S(1)} %copy-done.4, s32[]{:T(128)} %bitcast.1, ...), kind=kLoop, calls=%fused_computation.86 | loop fusion | flops 98304 | bytes 442400 | tf_op jit(solution)/shard_map/add | solution.py:23
  33.3 14.2 %subtract_convert_fusion = (bf16[96,128,384]{2,1,0:T(8,128)(2,1)}, bf16[96,128,384]{2,1,0:T(8,128)(2,1)}) fusion(bf16[96,128,512]{2,1,0:T(8,128)(2,1)} %reshape.165, f32[96,128]{1,0:T(8,128)S(1)} %bitcast.120, s32[96,128]{1,0:T(8,128)S(1)} %get-tuple-element.32, f32[96,128]{1,0:T(8,128)S(1)} %bitcast.122, s32[96,128]{1,0:T(8,128)S(1)} %get-tuple-element.33, ...), kind=kOutput, calls=%fused_computation.5 | convolution fusion | flops 1264582656 | bytes 29097984 | tf_op jit(solution)/shard_map/bcr,brf->bcf/dot_general | solution.py:62
  47.5 15.3 %pad_maximum_fusion = bf16[192,128,384]{2,1,0:T(8,128)(2,1)} fusion(bf16[96,128,384]{2,1,0:T(8,128)(2,1)} %get-tuple-element.10, bf16[96,128,384]{2,1,0:T(8,128)(2,1)} %get-tuple-element.11), kind=kLoop, calls=%fused_computation.2 | loop fusion | flops 9437184 | bytes 37748736 | tf_op jit(solution)/shard_map/concatenate | solution.py:68
  62.8 30.0 %fusion.3 = bf16[152,128,384]{2,0,1:T(8,128)(2,1)} fusion(bf16[192,128,384]{2,1,0:T(8,128)(2,1)} %pad_maximum_fusion, pred[152,96]{1,0:T(8,128)(4,1)S(1)} %iota_compare_fusion.8), kind=kOutput, calls=%fused_computation.8 | convolution fusion | flops 2876404224 | bytes 33831168 | tf_op jit(solution)/shard_map/sb,bcf->scf/dot_general | solution.py:65
  92.8 11.9 %copy.27 = bf16[152,128,384]{2,1,0:T(8,128)(2,1)} copy(bf16[152,128,384]{2,0,1:T(8,128)(2,1)} %fusion.3) | data formatting | bytes 29884416 | tf_op jit(solution)/shard_map/convert_element_type | solution.py:70
  104.6 7.6 %dynamic-slice_bitcast_fusion = bf16[4,19,128,384]{3,2,1,0:T(8,128)(2,1)} fusion(bf16[2,4,19,128,384]{4,3,2,1,0:T(8,128)(2,1)} %bitcast.97, s32[]{:T(128)S(6)} %select_n.123), kind=kLoop, calls=%fused_computation.12 | loop fusion | bytes 14942212 | tf_op jit(solution)/shard_map/jit(dynamic_index_in_dim)/squeeze | solution.py:73
  112.7 11.8 %collective-permute-done = bf16[4,19,128,384]{3,2,1,0:T(8,128)(2,1)} collective-permute-done((bf16[4,19,128,384]{3,2,1,0:T(8,128)(2,1)}, bf16[4,19,128,384]{3,2,1,0:T(8,128)(2,1)}, u32[]{:S(2)}, u32[]{:S(2)}) %collective-permute-start) | collective-permute-done | bytes 7471136 | tf_op jit(solution)/shard_map/ppermute | solution.py:76
  124.5 11.9 %fusion.2 = bf16[4,19,128,384]{3,2,1,0:T(8,128)(2,1)} fusion(bf16[4,19,128,384]{3,2,1,0:T(8,128)(2,1)} %collective-permute-done, bf16[2,4,19,128,384]{4,3,2,1,0:T(8,128)(2,1)} %bitcast.98, s32[]{:T(128)S(6)} %select_n.118), kind=kLoop, calls=%fused_computation.7 | loop fusion | flops 14942208 | bytes 22413316 | tf_op jit(solution)/shard_map/convert_element_type | solution.py:77
  136.5 5.5 %dynamic-slice_bitcast_fusion.4 = (bf16[19,128,384]{2,1,0:T(8,128)(2,1)}, bf16[19,128,384]{2,1,0:T(8,128)(2,1)}, bf16[19,128,384]{2,1,0:T(8,128)(2,1)}) fusion(bf16[4,19,128,384]{3,2,1,0:T(8,128)(2,1)} %fusion.2, s32[]{:T(128)S(6)} %select_n.124, s32[]{:T(128)S(6)} %select_n.126, s32[]{:T(128)S(6)} %select_n.125), kind=kLoop, calls=%fused_computation.57 | loop fusion | bytes 11206668 | tf_op jit(solution)/shard_map/jit(dynamic_index_in_dim)/squeeze | solution.py:92
  146.4 10.0 %subtract_convert_fusion.1 = (bf16[96,128,128]{2,1,0:T(8,128)(2,1)S(1)}, bf16[96,128,128]{2,1,0:T(8,128)(2,1)}) fusion(bf16[96,128,512]{2,1,0:T(8,128)(2,1)} %reshape.165, f32[96,128]{1,0:T(8,128)S(1)} %bitcast.121, s32[96,128]{1,0:T(8,128)S(1)} %copy-done.20, f32[96,128]{1,0:T(8,128)S(1)} %bitcast.123, s32[96,128]{1,0:T(8,128)S(1)} %copy-done.22, ...), kind=kOutput, calls=%fused_computation.16 | convolution fusion | flops 446693376 | bytes 10223616 | tf_op jit(solution)/shard_map/bcr,brf->bcf/dot_general | solution.py:62
  158.9 4.7 %fusion.23 = bf16[152,128,128]{2,0,1:T(8,128)(2,1)S(1)} fusion(bf16[192,128,128]{2,1,0:T(8,128)(2,1)S(1)} %pad_maximum_fusion.1, pred[152,96]{1,0:T(8,128)(4,1)S(1)} %iota_compare_fusion.8), kind=kOutput, calls=%fused_computation.48 | convolution fusion | flops 958820864 | bytes 11286784 | tf_op jit(solution)/shard_map/sb,bcf->scf/dot_general | solution.py:65
  167.0 19.7 %collective-permute-done.1 = bf16[19,128,384]{2,1,0:T(8,128)(2,1)} collective-permute-done((bf16[19,128,384]{2,1,0:T(8,128)(2,1)}, bf16[19,128,384]{2,1,0:T(8,128)(2,1)}, u32[]{:S(2)}, u32[]{:S(2)}) %collective-permute-start.1) | collective-permute-done | bytes 1867808 | tf_op jit(solution)/shard_map/ppermute | solution.py:93
  186.7 40.9 %collective-permute-done.2 = bf16[19,128,384]{2,1,0:T(8,128)(2,1)} collective-permute-done((bf16[19,128,384]{2,1,0:T(8,128)(2,1)}, bf16[19,128,384]{2,1,0:T(8,128)(2,1)}, u32[]{:S(2)}, u32[]{:S(2)}) %collective-permute-start.2) | collective-permute-done | bytes 1867808 | tf_op jit(solution)/shard_map/ppermute | solution.py:93
  227.6 5.2 %fusion.20 = bf16[19,128,384]{2,1,0:T(8,128)(2,1)S(1)} fusion(bf16[19,128,384]{2,1,0:T(8,128)(2,1)} %collective-permute-done.3, bf16[19,128,384]{2,1,0:T(8,128)(2,1)} %collective-permute-done.2, bf16[19,128,384]{2,1,0:T(8,128)(2,1)} %collective-permute-done.1, bf16[4,19,128,384]{3,2,1,0:T(8,128)(2,1)} %collective-permute-done, s32[]{:T(128)S(6)} %select_n.121, ...), kind=kLoop, calls=%fused_computation.44 | loop fusion | flops 9338880 | bytes 11206668 | tf_op jit(solution)/shard_map/convert_element_type | solution.py:97
  233.0 17.7 %multiply_convert_fusion.1 = (bf16[1024,1024]{1,0:T(8,128)(2,1)S(1)}, bf16[1024,1024]{1,0:T(8,128)(2,1)S(1)}, bf16[1024,1024]{1,0:T(8,128)(2,1)S(1)}) fusion(f32[1024]{0:T(1024)S(1)} %subtract_multiply_fusion), kind=kLoop, calls=%fused_computation.35 | loop fusion | flops 22020096 | bytes 6295552 | tf_op jit(solution)/shard_map/convert.20
  250.7 36.9 %maximum_maximum_fusion = bf16[2048,2048]{1,0:T(8,128)(2,1)} fusion(bf16[1024,1024]{1,0:T(8,128)(2,1)S(1)} %get-tuple-element.36, bf16[1024,1024]{1,0:T(8,128)(2,1)S(1)} %get-tuple-element.35, bf16[1024,1024]{1,0:T(8,128)(2,1)S(1)} %get-tuple-element.34), kind=kLoop, calls=%fused_computation.11 | loop fusion | flops 33554432 | bytes 14680064 | tf_op jit(solution)/shard_map/concatenate | solution.py:43
  290.1 5.1 %all-to-all-start = ((bf16[19,128,384]{2,0,1:T(8,128)(2,1)}), bf16[19,128,384]{2,0,1:T(8,128)(2,1)S(1)}, u32[]{:S(2)}, u32[]{:S(2)}) async-start(bf16[19,128,384]{2,0,1:T(8,128)(2,1)} %copy.28), calls=%async_computation | async-start | bytes 4718592 | tf_op jit(solution)/shard_map/all_to_all | solution.py:135
  306.5 8.3 %copy.30 = bf16[4,2,256,2048]{3,2,1,0:T(8,128)(2,1)} copy(bf16[4,2,256,2048]{3,2,0,1:T(8,128)(2,1)} %bitcast.102) | data formatting | bytes 16777216 | tf_op jit(solution)/shard_map/transpose | solution.py:131
  314.8 6.5 %slice.109 = bf16[4,384,2048]{2,1,0:T(8,128)(2,1)} slice(bf16[4,512,2048]{2,1,0:T(8,128)(2,1)} %bitcast.103), slice={[0:4], [0:384], [0:2048]} | slice | bytes 12582912 | tf_op jit(solution)/shard_map/slice | solution.py:137
  324.5 25.1 %all-to-all-done = bf16[19,128,384]{2,0,1:T(8,128)(2,1)S(1)} async-done(((bf16[19,128,384]{2,0,1:T(8,128)(2,1)}), bf16[19,128,384]{2,0,1:T(8,128)(2,1)S(1)}, u32[]{:S(2)}, u32[]{:S(2)}) %all-to-all-start) | async-done | bytes 1867808 | tf_op jit(solution)/shard_map/all_to_all | solution.py:135
  360.0 9.8 %fusion.42 = f32[608,2048]{1,0:T(8,128)} fusion(bf16[608,1536]{1,0:T(8,128)(2,1)} %bitcast.116, bf16[1536,2048]{1,0:T(8,128)(2,1)} %bitcast.113), kind=kOutput, calls=%fused_computation.104 | convolution fusion | flops 3825205248 | bytes 13139968 | tf_op jit(solution)/shard_map/dot_general | solution.py:138
  369.8 10.0 %all-to-all-done.1 = bf16[19,128,128]{2,0,1:T(8,128)(2,1)S(1)} async-done(((bf16[19,128,128]{2,0,1:T(8,128)(2,1)}), bf16[19,128,128]{2,0,1:T(8,128)(2,1)S(1)}, u32[]{:S(2)}, u32[]{:S(2)}) %all-to-all-start.1) | async-done | bytes 622624 | tf_op jit(solution)/shard_map/all_to_all | solution.py:135
  385.9 4.6 %collective-permute-done.8 = f32[19,1024]{1,0:T(8,128)S(1)} collective-permute-done((f32[19,1024]{1,0:T(8,128)S(1)}, f32[19,1024]{1,0:T(8,128)S(1)}, u32[]{:S(2)}, u32[]{:S(2)}) %collective-permute-start.8) | collective-permute-done | bytes 77856 | tf_op jit(solution)/shard_map/ppermute | solution.py:55
  (100 shorter events, 57.9 us)
Async XLA Ops:
  4.7 28.6 %copy-start.5 = (f32[96,1,128]{2,1,0:T(1,128)}, f32[96,1,128]{2,1,0:T(1,128)S(1)}, u32[]{:S(2)}) copy-start(f32[96,1,128]{2,1,0:T(1,128)S(1)} %get-tuple-element.25) | copy-start | bytes 147460
  4.7 20.5 %copy-start.23 = (s32[96]{0:T(128)S(1)}, s32[96]{0:T(128)}, u32[]{:S(2)}) copy-start(s32[96]{0:T(128)} %param.11) | copy-start | bytes 1156
  4.7 20.5 %copy-start = (s32[80]{0:T(128)S(1)}, s32[80]{0:T(128)}, u32[]{:S(2)}) copy-start(s32[80]{0:T(128)} %param.12) | copy-start | bytes 964
  4.7 23.4 %copy-start.4 = (s32[12288]{0:T(1024)S(1)}, s32[12288]{0:T(1024)}, u32[]{:S(2)}) copy-start(s32[12288]{0:T(1024)} %param.8) | copy-start | bytes 147460
  33.2 14.3 %copy-start.7 = (s32[96,128]{1,0:T(8,128)}, s32[96,128]{1,0:T(8,128)S(1)}, u32[]{:S(2)}) copy-start(s32[96,128]{1,0:T(8,128)S(1)} %get-tuple-element.26) | copy-start | bytes 147460
  33.2 14.3 %copy-start.9 = (s32[96,128]{1,0:T(8,128)}, s32[96,128]{1,0:T(8,128)S(1)}, u32[]{:S(2)}) copy-start(s32[96,128]{1,0:T(8,128)S(1)} %get-tuple-element.27) | copy-start | bytes 147460
  33.2 14.2 %copy-start.11 = (s32[96,128]{1,0:T(8,128)}, s32[96,128]{1,0:T(8,128)S(1)}, u32[]{:S(2)}) copy-start(s32[96,128]{1,0:T(8,128)S(1)} %get-tuple-element.28) | copy-start | bytes 147460
  33.2 14.2 %copy-start.13 = (s32[96,128]{1,0:T(8,128)}, s32[96,128]{1,0:T(8,128)S(1)}, u32[]{:S(2)}) copy-start(s32[96,128]{1,0:T(8,128)S(1)} %get-tuple-element.29) | copy-start | bytes 147460
  33.2 14.2 %copy-start.15 = (s32[96,128]{1,0:T(8,128)}, s32[96,128]{1,0:T(8,128)S(1)}, u32[]{:S(2)}) copy-start(s32[96,128]{1,0:T(8,128)S(1)} %get-tuple-element.30) | copy-start | bytes 147460
  33.2 14.2 %copy-start.17 = (s32[96,128]{1,0:T(8,128)}, s32[96,128]{1,0:T(8,128)S(1)}, u32[]{:S(2)}) copy-start(s32[96,128]{1,0:T(8,128)S(1)} %get-tuple-element.31) | copy-start | bytes 147460
  112.2 12.3 %collective-permute-start = (bf16[4,19,128,384]{3,2,1,0:T(8,128)(2,1)}, bf16[4,19,128,384]{3,2,1,0:T(8,128)(2,1)}, u32[]{:S(2)}, u32[]{:S(2)}) collective-permute-start(bf16[4,19,128,384]{3,2,1,0:T(8,128)(2,1)} %dynamic-slice_bitcast_fusion), channel_id=1, source_target_pairs={{0,4},{4,0},{8,12},{12,8},{16,20},{20,16},{24,28},{28,24},{1,5},{5... | collective-permute-start | bytes 22413320 | tf_op jit(solution)/shard_map/ppermute | solution.py:76
  142.0 44.7 %collective-permute-start.1 = (bf16[19,128,384]{2,1,0:T(8,128)(2,1)}, bf16[19,128,384]{2,1,0:T(8,128)(2,1)}, u32[]{:S(2)}, u32[]{:S(2)}) collective-permute-start(bf16[19,128,384]{2,1,0:T(8,128)(2,1)} %get-tuple-element.12), channel_id=1, source_target_pairs={{0,8},{4,12},{8,0},{12,4},{16,24},{20,28},{24,16},{28,20},{1,9},{5... | collective-permute-start | bytes 5603336 | tf_op jit(solution)/shard_map/ppermute | solution.py:93
  144.8 82.8 %collective-permute-start.2 = (bf16[19,128,384]{2,1,0:T(8,128)(2,1)}, bf16[19,128,384]{2,1,0:T(8,128)(2,1)}, u32[]{:S(2)}, u32[]{:S(2)}) collective-permute-start(bf16[19,128,384]{2,1,0:T(8,128)(2,1)} %get-tuple-element.14), channel_id=1, source_target_pairs={{0,16},{4,20},{8,24},{12,28},{16,0},{20,4},{24,8},{28,12},{1,17},{... | collective-permute-start | bytes 5603336 | tf_op jit(solution)/shard_map/ppermute | solution.py:93
  146.3 81.3 %collective-permute-start.3 = (bf16[19,128,384]{2,1,0:T(8,128)(2,1)}, bf16[19,128,384]{2,1,0:T(8,128)(2,1)}, u32[]{:S(2)}, u32[]{:S(2)}) collective-permute-start(bf16[19,128,384]{2,1,0:T(8,128)(2,1)} %get-tuple-element.13), channel_id=1, source_target_pairs={{0,24},{4,28},{8,16},{12,20},{16,8},{20,12},{24,0},{28,4},{1,25},{... | collective-permute-start | bytes 5603336 | tf_op jit(solution)/shard_map/ppermute | solution.py:93
  164.9 68.0 %copy-start.1 = (bf16[152,128,128]{2,1,0:T(8,128)(2,1)}, bf16[152,128,128]{2,1,0:T(8,128)(2,1)S(1)}, u32[]{:S(2)}) copy-start(bf16[152,128,128]{2,1,0:T(8,128)(2,1)S(1)} %copy.32) | copy-start | bytes 14942212
  232.9 62.4 %collective-permute-start.4 = (bf16[4,19,128,128]{3,2,1,0:T(8,128)(2,1)}, bf16[4,19,128,128]{3,2,1,0:T(8,128)(2,1)}, u32[]{:S(2)}, u32[]{:S(2)}) collective-permute-start(bf16[4,19,128,128]{3,2,1,0:T(8,128)(2,1)} %dynamic-slice_bitcast_fusion.1), channel_id=1, source_target_pairs={{0,4},{4,0},{8,12},{12,8},{16,20},{20,16},{24,28},{28,24},{1,5},{5... | collective-permute-start | bytes 7471112 | tf_op jit(solution)/shard_map/ppermute | solution.py:76
  290.1 59.5 %all-to-all-start = ((bf16[19,128,384]{2,0,1:T(8,128)(2,1)}), bf16[19,128,384]{2,0,1:T(8,128)(2,1)S(1)}, u32[]{:S(2)}, u32[]{:S(2)}) async-start(bf16[19,128,384]{2,0,1:T(8,128)(2,1)} %copy.28), calls=%async_computation | async-start | bytes 4718592 | tf_op jit(solution)/shard_map/all_to_all | solution.py:135
  300.1 52.7 %collective-permute-start.5 = (bf16[19,128,128]{2,1,0:T(8,128)(2,1)}, bf16[19,128,128]{2,1,0:T(8,128)(2,1)S(1)}, u32[]{:S(2)}, u32[]{:S(2)}) collective-permute-start(bf16[19,128,128]{2,1,0:T(8,128)(2,1)} %get-tuple-element.15), channel_id=1, source_target_pairs={{0,8},{4,12},{8,0},{12,4},{16,24},{20,28},{24,16},{28,20},{1,9},{5... | collective-permute-start | bytes 1867784 | tf_op jit(solution)/shard_map/ppermute | solution.py:93
  301.3 51.4 %collective-permute-start.6 = (bf16[19,128,128]{2,1,0:T(8,128)(2,1)}, bf16[19,128,128]{2,1,0:T(8,128)(2,1)}, u32[]{:S(2)}, u32[]{:S(2)}) collective-permute-start(bf16[19,128,128]{2,1,0:T(8,128)(2,1)} %get-tuple-element.17), channel_id=1, source_target_pairs={{0,16},{4,20},{8,24},{12,28},{16,0},{20,4},{24,8},{28,12},{1,17},{... | collective-permute-start | bytes 1867784 | tf_op jit(solution)/shard_map/ppermute | solution.py:93
  302.2 50.6 %collective-permute-start.7 = (bf16[19,128,128]{2,1,0:T(8,128)(2,1)}, bf16[19,128,128]{2,1,0:T(8,128)(2,1)}, u32[]{:S(2)}, u32[]{:S(2)}) collective-permute-start(bf16[19,128,128]{2,1,0:T(8,128)(2,1)} %get-tuple-element.16), channel_id=1, source_target_pairs={{0,24},{4,28},{8,16},{12,20},{16,8},{20,12},{24,0},{28,4},{1,25},{... | collective-permute-start | bytes 1867784 | tf_op jit(solution)/shard_map/ppermute | solution.py:93
  356.3 23.5 %all-to-all-start.1 = ((bf16[19,128,128]{2,0,1:T(8,128)(2,1)}), bf16[19,128,128]{2,0,1:T(8,128)(2,1)S(1)}, u32[]{:S(2)}, u32[]{:S(2)}) async-start(bf16[19,128,128]{2,0,1:T(8,128)(2,1)} %copy.33), calls=%async_computation.1 | async-start | bytes 1572864 | tf_op jit(solution)/shard_map/all_to_all | solution.py:135
  360.0 20.3 %copy-start.2 = (bf16[4,128,2048]{2,1,0:T(8,128)(2,1)S(1)}, bf16[4,128,2048]{2,1,0:T(8,128)(2,1)}, u32[]{:S(2)}) copy-start(bf16[4,128,2048]{2,1,0:T(8,128)(2,1)} %slice.111) | copy-start | bytes 6291460
  385.8 4.7 %collective-permute-start.8 = (f32[19,1024]{1,0:T(8,128)S(1)}, f32[19,1024]{1,0:T(8,128)S(1)}, u32[]{:S(2)}, u32[]{:S(2)}) collective-permute-start(f32[19,1024]{1,0:T(8,128)S(1)} %fusion.27), channel_id=1, source_target_pairs={{0,1},{1,0},{2,3},{3,2},{4,5},{5,4},{6,7},{7,6},{8,9},{9,8},{10,11... | collective-permute-start | bytes 233480 | tf_op jit(solution)/shard_map/ppermute | solution.py:55
  390.5 6.1 %collective-permute-start.9 = (f32[19,1024]{1,0:T(8,128)S(1)}, f32[19,1024]{1,0:T(8,128)S(1)}, u32[]{:S(2)}, u32[]{:S(2)}) collective-permute-start(f32[19,1024]{1,0:T(8,128)S(1)} %add.327), channel_id=1, source_target_pairs={{0,2},{1,3},{2,0},{3,1},{4,6},{5,7},{6,4},{7,5},{8,10},{9,11},{10,... | collective-permute-start | bytes 233480 | tf_op jit(solution)/shard_map/ppermute | solution.py:55
  (14 other events, 135.1 us)
where the time goes:
time: 404 us; the launch traced here: 398 us
  waiting for transfers between devices  116 us (29%)
  other arithmetic  110 us (27%)
  local copies, waits for them, and re-layouts  79.8 us (20%)
  matrix products  72.8 us (18%)
  starting transfers between devices  17.4 us (4%)
    ppermute x6, waiting for transfers between devices, _scatter_pairs(): lax.ppermute(send, 'uv', _partner_pairs(n_owners, lambda i, dest=dest: de...  60.7 us
    concatenate x1, other arithmetic, delay_table(): return jnp.concatenate([upper, lower], axis=0).astype(jnp.bfloat16)  36.9 us
    all_to_all x2, waiting for transfers between devices, body(): lax.all_to_all(gridded, 'chan', split_axis=1, concat_axis=2, tiled=True)  35.1 us
    dot_general x2, matrix products, _gather_pair(): jnp.einsum('sb,bcf->scf', pick2, jnp.concatenate([high, low], axis=0), pr...  34.7 us
    dot_general x2, matrix products, _gather_pair(): jnp.einsum('bcr,brf->bcf', matrix, part, preferred_element_type=jnp.float32)  24.2 us
    reshape x1, local copies, waits for them, and re-layouts, body(): blocks = vis.reshape(nblocks, BR, width)  20.5 us
    concatenate x2, other arithmetic, _gather_pair(): jnp.concatenate([high, low], axis=0)  17.7 us
    another operation x1, other arithmetic  17.7 us
  transfers between devices with their start and end apart: 12, of which 7 were waited for; matrix products, arithmetic and copies ran while one was open for 30% of the time, Pallas kernels for 0%

commit v1 on v0

--- a/solution.py
+++ b/solution.py
@@ -132,7 +132,19 @@
     by_source = by_source.reshape(n_chan, width, 2 * CH)
     out = None
     for gridded, lo, hi in ((first_grid, 0, cut), (second_grid, cut, width)):
-        piece = lax.all_to_all(gridded, "chan", split_axis=1, concat_axis=2, tiled=True)
+
+        def match_surface_in(local, peer_axis, in_dim, dim_k):
+            return jnp.concatenate(
+                lax.all_to_all(
+                    jnp.stack(jnp.split(local, lax.psum(1, peer_axis), axis=in_dim), axis=0),
+                    peer_axis,
+                    0,
+                    0,
+                ),
+                axis=dim_k,
+            )
+
+        piece = match_surface_in(gridded, "chan", 1, 2)
         count, cells_part = (piece.shape[0], piece.shape[1])
         rows = by_source[:, lo:hi, :].reshape(n_chan * (hi - lo), 2 * CH)
         term = jnp.dot(

time: 404 us -> 372 us (0.921)
  waiting for transfers between devices: 116 us -> 86.3 us
  local copies, waits for them, and re-layouts: 79.8 us -> 75.7 us
    ppermute x6, waiting for transfers between devices: 60.7 us -> 43 us  [_scatter_pairs(): lax.ppermute(send, 'uv', _partner_pairs(n_owners, lambda i, dest=dest: de...]
    all_to_all x2, waiting for transfers between devices: 35.1 us -> 22.7 us  [match_surface_in(): lax.all_to_all(jnp.stack(jnp.split(local, lax.psum(1, peer_axis), axis=in...]
    another operation x1 -> x3, other arithmetic: 17.7 us -> 20.1 us
  transfers between devices with their start and end apart: 12 -> 12, of which waited for: 7 -> 7; matrix products, arithmetic and copies ran while one was open for 30% -> 32% of each run, Pallas kernels for 0% -> 0%
where the time goes in v1:
time: 372 us; the launch traced here: 366 us
  other arithmetic  113 us (30%)
  waiting for transfers between devices  86.3 us (23%)
  local copies, waits for them, and re-layouts  75.7 us (20%)
  matrix products  72.6 us (20%)
  starting transfers between devices  17.1 us (5%)
    ppermute x6, waiting for transfers between devices, _scatter_pairs(): lax.ppermute(send, 'uv', _partner_pairs(n_owners, lambda i, dest=dest: de...  43 us
    concatenate x1, other arithmetic, delay_table(): return jnp.concatenate([upper, lower], axis=0).astype(jnp.bfloat16)  36.8 us
    dot_general x2, matrix products, _gather_pair(): jnp.einsum('sb,bcf->scf', pick2, jnp.concatenate([high, low], axis=0), pr...  34.7 us
    dot_general x2, matrix products, _gather_pair(): jnp.einsum('bcr,brf->bcf', matrix, part, preferred_element_type=jnp.float32)  24.2 us
    all_to_all x2, waiting for transfers between devices, match_surface_in(): lax.all_to_all(jnp.stack(jnp.split(local, lax.psum(1, peer_axis), axis=in...  22.7 us
    reshape x1, local copies, waits for them, and re-layouts, body(): blocks = vis.reshape(nblocks, BR, width)  20.5 us
    concatenate x2, other arithmetic, _gather_pair(): jnp.concatenate([high, low], axis=0)  18 us
    another operation x1, other arithmetic  17.6 us
  transfers between devices with their start and end apart: 12, of which 7 were waited for; matrix products, arithmetic and copies ran while one was open for 32% of the time, Pallas kernels for 0%

profile of v1, /device:TPU:0, one launch (start us, length us, event | category | flops | bytes accessed | tf_op | source)
XLA Modules:
  0.0 365.6 jit_solution(5586144388246204806)
XLA Ops:
  4.7 20.5 %reshape.163 = bf16[96,128,512]{2,1,0:T(8,128)(2,1)} reshape(bf16[12288,2,256]{2,1,0:T(2,128)(2,1)} %param.7) | data formatting | bytes 25165824 | tf_op jit(solution)/shard_map/reshape | solution.py:118
  28.1 5.1 %add_bitcast_fusion.10 = (s32[96,128]{1,0:T(8,128)S(1)}, s32[96,128]{1,0:T(8,128)S(1)}, s32[96,128]{1,0:T(8,128)S(1)}, s32[96,128]{1,0:T(8,128)S(1)}, s32[96,128...) fusion(s32[12288]{0:T(1024)S(1)} %copy-done.4, s32[]{:T(128)} %bitcast.1, ...), kind=kLoop, calls=%fused_computation.96 | loop fusion | flops 98304 | bytes 442400 | tf_op jit(solution)/shard_map/add | solution.py:23
  33.3 14.2 %subtract_convert_fusion = (bf16[96,128,384]{2,1,0:T(8,128)(2,1)}, bf16[96,128,384]{2,1,0:T(8,128)(2,1)}) fusion(bf16[96,128,512]{2,1,0:T(8,128)(2,1)} %reshape.163, f32[96,128]{1,0:T(8,128)S(1)} %bitcast.133, s32[96,128]{1,0:T(8,128)S(1)} %get-tuple-element.40, f32[96,128]{1,0:T(8,128)S(1)} %bitcast.135, s32[96,128]{1,0:T(8,128)S(1)} %get-tuple-element.41, ...), kind=kOutput, calls=%fused_computation.5 | convolution fusion | flops 1264582656 | bytes 29097984 | tf_op jit(solution)/shard_map/bcr,brf->bcf/dot_general | solution.py:62
  47.5 15.5 %pad_maximum_fusion = bf16[192,128,384]{2,1,0:T(8,128)(2,1)} fusion(bf16[96,128,384]{2,1,0:T(8,128)(2,1)} %get-tuple-element.10, bf16[96,128,384]{2,1,0:T(8,128)(2,1)} %get-tuple-element.11), kind=kLoop, calls=%fused_computation.2 | loop fusion | flops 9437184 | bytes 37748736 | tf_op jit(solution)/shard_map/concatenate | solution.py:68
  63.1 30.0 %fusion.3 = bf16[152,128,384]{2,0,1:T(8,128)(2,1)} fusion(bf16[192,128,384]{2,1,0:T(8,128)(2,1)} %pad_maximum_fusion, pred[152,96]{1,0:T(8,128)(4,1)S(1)} %iota_compare_fusion.8), kind=kOutput, calls=%fused_computation.8 | convolution fusion | flops 2876404224 | bytes 33831168 | tf_op jit(solution)/shard_map/sb,bcf->scf/dot_general | solution.py:65
  93.0 12.0 %copy.20 = bf16[152,128,384]{2,1,0:T(8,128)(2,1)} copy(bf16[152,128,384]{2,0,1:T(8,128)(2,1)} %fusion.3) | data formatting | bytes 29884416 | tf_op jit(solution)/shard_map/convert_element_type | solution.py:70
  105.1 7.6 %dynamic-slice_bitcast_fusion = bf16[4,19,128,384]{3,2,1,0:T(8,128)(2,1)} fusion(bf16[2,4,19,128,384]{4,3,2,1,0:T(8,128)(2,1)} %bitcast.111, s32[]{:T(128)S(6)} %select_n.123), kind=kLoop, calls=%fused_computation.12 | loop fusion | bytes 14942212 | tf_op jit(solution)/shard_map/jit(dynamic_index_in_dim)/squeeze | solution.py:73
  113.1 11.8 %collective-permute-done = bf16[4,19,128,384]{3,2,1,0:T(8,128)(2,1)} collective-permute-done((bf16[4,19,128,384]{3,2,1,0:T(8,128)(2,1)}, bf16[4,19,128,384]{3,2,1,0:T(8,128)(2,1)}, u32[]{:S(2)}, u32[]{:S(2)}) %collective-permute-start) | collective-permute-done | bytes 7471136 | tf_op jit(solution)/shard_map/ppermute | solution.py:76
  125.0 11.9 %fusion.2 = bf16[4,19,128,384]{3,2,1,0:T(8,128)(2,1)} fusion(bf16[4,19,128,384]{3,2,1,0:T(8,128)(2,1)} %collective-permute-done, bf16[2,4,19,128,384]{4,3,2,1,0:T(8,128)(2,1)} %bitcast.112, s32[]{:T(128)S(6)} %select_n.118), kind=kLoop, calls=%fused_computation.7 | loop fusion | flops 14942208 | bytes 22413316 | tf_op jit(solution)/shard_map/convert_element_type | solution.py:77
  136.9 5.5 %dynamic-slice_bitcast_fusion.4 = (bf16[19,128,384]{2,1,0:T(8,128)(2,1)}, bf16[19,128,384]{2,1,0:T(8,128)(2,1)}, bf16[19,128,384]{2,1,0:T(8,128)(2,1)}) fusion(bf16[4,19,128,384]{3,2,1,0:T(8,128)(2,1)} %fusion.2, s32[]{:T(128)S(6)} %select_n.124, s32[]{:T(128)S(6)} %select_n.126, s32[]{:T(128)S(6)} %select_n.125), kind=kLoop, calls=%fused_computation.58 | loop fusion | bytes 11206668 | tf_op jit(solution)/shard_map/jit(dynamic_index_in_dim)/squeeze | solution.py:92
  146.8 10.0 %subtract_convert_fusion.1 = (bf16[96,128,128]{2,1,0:T(8,128)(2,1)S(1)}, bf16[96,128,128]{2,1,0:T(8,128)(2,1)}) fusion(bf16[96,128,512]{2,1,0:T(8,128)(2,1)} %reshape.163, f32[96,128]{1,0:T(8,128)S(1)} %bitcast.134, s32[96,128]{1,0:T(8,128)S(1)} %copy-done.20, f32[96,128]{1,0:T(8,128)S(1)} %bitcast.136, s32[96,128]{1,0:T(8,128)S(1)} %copy-done.22, ...), kind=kOutput, calls=%fused_computation.16 | convolution fusion | flops 446693376 | bytes 10223616 | tf_op jit(solution)/shard_map/bcr,brf->bcf/dot_general | solution.py:62
  159.3 4.7 %fusion.23 = bf16[152,128,128]{2,0,1:T(8,128)(2,1)S(1)} fusion(bf16[192,128,128]{2,1,0:T(8,128)(2,1)S(1)} %pad_maximum_fusion.1, pred[152,96]{1,0:T(8,128)(4,1)S(1)} %iota_compare_fusion.8), kind=kOutput, calls=%fused_computation.48 | convolution fusion | flops 958820864 | bytes 11286784 | tf_op jit(solution)/shard_map/sb,bcf->scf/dot_general | solution.py:65
  167.4 17.6 %multiply_convert_fusion.1 = (bf16[1024,1024]{1,0:T(8,128)(2,1)S(1)}, bf16[1024,1024]{1,0:T(8,128)(2,1)S(1)}, bf16[1024,1024]{1,0:T(8,128)(2,1)S(1)}) fusion(f32[1024]{0:T(1024)S(1)} %subtract_multiply_fusion), kind=kLoop, calls=%fused_computation.35 | loop fusion | flops 22020096 | bytes 6295552 | tf_op jit(solution)/shard_map/convert.20
  187.1 40.9 %collective-permute-done.2 = bf16[19,128,384]{2,1,0:T(8,128)(2,1)} collective-permute-done((bf16[19,128,384]{2,1,0:T(8,128)(2,1)}, bf16[19,128,384]{2,1,0:T(8,128)(2,1)}, u32[]{:S(2)}, u32[]{:S(2)}) %collective-permute-start.2) | collective-permute-done | bytes 1867808 | tf_op jit(solution)/shard_map/ppermute | solution.py:93
  228.1 5.3 %fusion.20 = bf16[19,128,384]{2,1,0:T(8,128)(2,1)S(1)} fusion(bf16[19,128,384]{2,1,0:T(8,128)(2,1)} %collective-permute-done.3, bf16[19,128,384]{2,1,0:T(8,128)(2,1)} %collective-permute-done.2, bf16[19,128,384]{2,1,0:T(8,128)(2,1)} %collective-permute-done.1, bf16[4,19,128,384]{3,2,1,0:T(8,128)(2,1)} %collective-permute-done, s32[]{:T(128)S(6)} %select_n.121, ...), kind=kLoop, calls=%fused_computation.44 | loop fusion | flops 9338880 | bytes 11206668 | tf_op jit(solution)/shard_map/convert_element_type | solution.py:97
  233.5 36.8 %maximum_maximum_fusion = bf16[2048,2048]{1,0:T(8,128)(2,1)} fusion(bf16[1024,1024]{1,0:T(8,128)(2,1)S(1)} %get-tuple-element.44, bf16[1024,1024]{1,0:T(8,128)(2,1)S(1)} %get-tuple-element.43, bf16[1024,1024]{1,0:T(8,128)(2,1)S(1)} %get-tuple-element.42), kind=kLoop, calls=%fused_computation.11 | loop fusion | flops 33554432 | bytes 14680064 | tf_op jit(solution)/shard_map/concatenate | solution.py:43
  272.0 5.1 %all-to-all-start = ((bf16[4,19,32,384]{3,2,1,0:T(8,128)(2,1)}), bf16[4,19,32,384]{3,2,1,0:T(8,128)(2,1)}, u32[]{:S(2)}, u32[]{:S(2)}) async-start(bf16[4,19,32,384]{3,2,1,0:T(8,128)(2,1)} %pad_maximum_fusion.2), calls=%async_computation | async-start | bytes 3735552 | tf_op jit(solution)/shard_map/all_to_all | solution.py:138
  288.5 8.3 %copy.22 = bf16[4,2,256,2048]{3,2,1,0:T(8,128)(2,1)} copy(bf16[4,2,256,2048]{3,2,0,1:T(8,128)(2,1)} %bitcast.116) | data formatting | bytes 16777216 | tf_op jit(solution)/shard_map/transpose | solution.py:131
  296.7 6.6 %slice.109 = bf16[4,384,2048]{2,1,0:T(8,128)(2,1)} slice(bf16[4,512,2048]{2,1,0:T(8,128)(2,1)} %bitcast.117), slice={[0:4], [0:384], [0:2048]} | slice | bytes 12582912 | tf_op jit(solution)/shard_map/slice | solution.py:149
  305.0 16.1 %all-to-all-done = bf16[4,19,32,384]{3,2,1,0:T(8,128)(2,1)} async-done(((bf16[4,19,32,384]{3,2,1,0:T(8,128)(2,1)}), bf16[4,19,32,384]{3,2,1,0:T(8,128)(2,1)}, u32[]{:S(2)}, u32[]{:S(2)}) %all-to-all-start) | async-done | bytes 1867808 | tf_op jit(solution)/shard_map/all_to_all | solution.py:138
  331.9 9.7 %fusion.42 = f32[608,2048]{1,0:T(8,128)} fusion(bf16[608,1536]{1,0:T(8,128)(2,1)} %bitcast.129, bf16[1536,2048]{1,0:T(8,128)(2,1)} %bitcast.126), kind=kOutput, calls=%fused_computation.114 | convolution fusion | flops 3825205248 | bytes 13139968 | tf_op jit(solution)/shard_map/dot_general | solution.py:150
  341.5 6.7 %all-to-all-done.1 = bf16[4,19,32,128]{3,2,1,0:T(8,128)(2,1)S(1)} async-done(((bf16[4,19,32,128]{3,2,1,0:T(8,128)(2,1)}), bf16[4,19,32,128]{3,2,1,0:T(8,128)(2,1)S(1)}, u32[]{:S(2)}, u32[]{:S(2)}) %all-to-all-start.1) | async-done | bytes 622624 | tf_op jit(solution)/shard_map/all_to_all | solution.py:138
  354.0 4.6 %collective-permute-done.8 = f32[19,1024]{1,0:T(8,128)S(1)} collective-permute-done((f32[19,1024]{1,0:T(8,128)S(1)}, f32[19,1024]{1,0:T(8,128)S(1)}, u32[]{:S(2)}, u32[]{:S(2)}) %collective-permute-start.8) | collective-permute-done | bytes 77856 | tf_op jit(solution)/shard_map/ppermute | solution.py:55
  360.6 4.2 %collective-permute-done.9 = f32[19,1024]{1,0:T(8,128)S(1)} collective-permute-done((f32[19,1024]{1,0:T(8,128)S(1)}, f32[19,1024]{1,0:T(8,128)S(1)}, u32[]{:S(2)}, u32[]{:S(2)}) %collective-permute-start.9) | collective-permute-done | bytes 77856 | tf_op jit(solution)/shard_map/ppermute | solution.py:55
  (102 shorter events, 53.6 us)
Async XLA Ops:
  4.7 28.6 %copy-start.5 = (f32[96,1,128]{2,1,0:T(1,128)}, f32[96,1,128]{2,1,0:T(1,128)S(1)}, u32[]{:S(2)}) copy-start(f32[96,1,128]{2,1,0:T(1,128)S(1)} %get-tuple-element.33) | copy-start | bytes 147460
  4.7 20.5 %copy-start.23 = (s32[96]{0:T(128)S(1)}, s32[96]{0:T(128)}, u32[]{:S(2)}) copy-start(s32[96]{0:T(128)} %param.11) | copy-start | bytes 1156
  4.7 20.5 %copy-start = (s32[80]{0:T(128)S(1)}, s32[80]{0:T(128)}, u32[]{:S(2)}) copy-start(s32[80]{0:T(128)} %param.12) | copy-start | bytes 964
  4.7 23.4 %copy-start.4 = (s32[12288]{0:T(1024)S(1)}, s32[12288]{0:T(1024)}, u32[]{:S(2)}) copy-start(s32[12288]{0:T(1024)} %param.8) | copy-start | bytes 147460
  33.2 14.3 %copy-start.7 = (s32[96,128]{1,0:T(8,128)}, s32[96,128]{1,0:T(8,128)S(1)}, u32[]{:S(2)}) copy-start(s32[96,128]{1,0:T(8,128)S(1)} %get-tuple-element.34) | copy-start | bytes 147460
  33.2 14.2 %copy-start.9 = (s32[96,128]{1,0:T(8,128)}, s32[96,128]{1,0:T(8,128)S(1)}, u32[]{:S(2)}) copy-start(s32[96,128]{1,0:T(8,128)S(1)} %get-tuple-element.35) | copy-start | bytes 147460
  33.2 14.2 %copy-start.11 = (s32[96,128]{1,0:T(8,128)}, s32[96,128]{1,0:T(8,128)S(1)}, u32[]{:S(2)}) copy-start(s32[96,128]{1,0:T(8,128)S(1)} %get-tuple-element.36) | copy-start | bytes 147460
  33.2 14.2 %copy-start.13 = (s32[96,128]{1,0:T(8,128)}, s32[96,128]{1,0:T(8,128)S(1)}, u32[]{:S(2)}) copy-start(s32[96,128]{1,0:T(8,128)S(1)} %get-tuple-element.37) | copy-start | bytes 147460
  33.2 14.2 %copy-start.15 = (s32[96,128]{1,0:T(8,128)}, s32[96,128]{1,0:T(8,128)S(1)}, u32[]{:S(2)}) copy-start(s32[96,128]{1,0:T(8,128)S(1)} %get-tuple-element.38) | copy-start | bytes 147460
  33.3 14.2 %copy-start.17 = (s32[96,128]{1,0:T(8,128)}, s32[96,128]{1,0:T(8,128)S(1)}, u32[]{:S(2)}) copy-start(s32[96,128]{1,0:T(8,128)S(1)} %get-tuple-element.39) | copy-start | bytes 147460
  33.3 14.2 %copy-start.19 = (s32[96,128]{1,0:T(8,128)}, s32[96,128]{1,0:T(8,128)S(1)}, u32[]{:S(2)}) copy-start(s32[96,128]{1,0:T(8,128)S(1)} %get-tuple-element.40) | copy-start | bytes 147460
  112.6 12.3 %collective-permute-start = (bf16[4,19,128,384]{3,2,1,0:T(8,128)(2,1)}, bf16[4,19,128,384]{3,2,1,0:T(8,128)(2,1)}, u32[]{:S(2)}, u32[]{:S(2)}) collective-permute-start(bf16[4,19,128,384]{3,2,1,0:T(8,128)(2,1)} %dynamic-slice_bitcast_fusion), channel_id=1, source_target_pairs={{0,4},{4,0},{8,12},{12,8},{16,20},{20,16},{24,28},{28,24},{1,5},{5... | collective-permute-start | bytes 22413320 | tf_op jit(solution)/shard_map/ppermute | solution.py:76
  142.4 44.7 %collective-permute-start.1 = (bf16[19,128,384]{2,1,0:T(8,128)(2,1)}, bf16[19,128,384]{2,1,0:T(8,128)(2,1)}, u32[]{:S(2)}, u32[]{:S(2)}) collective-permute-start(bf16[19,128,384]{2,1,0:T(8,128)(2,1)} %get-tuple-element.12), channel_id=1, source_target_pairs={{0,8},{4,12},{8,0},{12,4},{16,24},{20,28},{24,16},{28,20},{1,9},{5... | collective-permute-start | bytes 5603336 | tf_op jit(solution)/shard_map/ppermute | solution.py:93
  145.2 82.8 %collective-permute-start.2 = (bf16[19,128,384]{2,1,0:T(8,128)(2,1)}, bf16[19,128,384]{2,1,0:T(8,128)(2,1)}, u32[]{:S(2)}, u32[]{:S(2)}) collective-permute-start(bf16[19,128,384]{2,1,0:T(8,128)(2,1)} %get-tuple-element.14), channel_id=1, source_target_pairs={{0,16},{4,20},{8,24},{12,28},{16,0},{20,4},{24,8},{28,12},{1,17},{... | collective-permute-start | bytes 5603336 | tf_op jit(solution)/shard_map/ppermute | solution.py:93
  146.8 81.3 %collective-permute-start.3 = (bf16[19,128,384]{2,1,0:T(8,128)(2,1)}, bf16[19,128,384]{2,1,0:T(8,128)(2,1)}, u32[]{:S(2)}, u32[]{:S(2)}) collective-permute-start(bf16[19,128,384]{2,1,0:T(8,128)(2,1)} %get-tuple-element.13), channel_id=1, source_target_pairs={{0,24},{4,28},{8,16},{12,20},{16,8},{20,12},{24,0},{28,4},{1,25},{... | collective-permute-start | bytes 5603336 | tf_op jit(solution)/shard_map/ppermute | solution.py:93
  165.3 68.1 %copy-start.1 = (bf16[152,128,128]{2,1,0:T(8,128)(2,1)}, bf16[152,128,128]{2,1,0:T(8,128)(2,1)S(1)}, u32[]{:S(2)}) copy-start(bf16[152,128,128]{2,1,0:T(8,128)(2,1)S(1)} %copy.24) | copy-start | bytes 14942212
  233.4 43.7 %collective-permute-start.4 = (bf16[4,19,128,128]{3,2,1,0:T(8,128)(2,1)}, bf16[4,19,128,128]{3,2,1,0:T(8,128)(2,1)S(1)}, u32[]{:S(2)}, u32[]{:S(2)}) collective-permute-start(bf16[4,19,128,128]{3,2,1,0:T(8,128)(2,1)} %dynamic-slice_bitcast_fusion.1), channel_id=1, source_target_pairs={{0,4},{4,0},{8,12},{12,8},{16,20},{20,16},{24,28},{28,24},{1,5},{5... | collective-permute-start | bytes 7471112 | tf_op jit(solution)/shard_map/ppermute | solution.py:76
  272.0 49.1 %all-to-all-start = ((bf16[4,19,32,384]{3,2,1,0:T(8,128)(2,1)}), bf16[4,19,32,384]{3,2,1,0:T(8,128)(2,1)}, u32[]{:S(2)}, u32[]{:S(2)}) async-start(bf16[4,19,32,384]{3,2,1,0:T(8,128)(2,1)} %pad_maximum_fusion.2), calls=%async_computation | async-start | bytes 3735552 | tf_op jit(solution)/shard_map/all_to_all | solution.py:138
  282.0 43.2 %collective-permute-start.5 = (bf16[19,128,128]{2,1,0:T(8,128)(2,1)}, bf16[19,128,128]{2,1,0:T(8,128)(2,1)S(1)}, u32[]{:S(2)}, u32[]{:S(2)}) collective-permute-start(bf16[19,128,128]{2,1,0:T(8,128)(2,1)} %get-tuple-element.15), channel_id=1, source_target_pairs={{0,8},{4,12},{8,0},{12,4},{16,24},{20,28},{24,16},{28,20},{1,9},{5... | collective-permute-start | bytes 1867784 | tf_op jit(solution)/shard_map/ppermute | solution.py:93
  283.3 42.0 %collective-permute-start.6 = (bf16[19,128,128]{2,1,0:T(8,128)(2,1)}, bf16[19,128,128]{2,1,0:T(8,128)(2,1)}, u32[]{:S(2)}, u32[]{:S(2)}) collective-permute-start(bf16[19,128,128]{2,1,0:T(8,128)(2,1)} %get-tuple-element.17), channel_id=1, source_target_pairs={{0,16},{4,20},{8,24},{12,28},{16,0},{20,4},{24,8},{28,12},{1,17},{... | collective-permute-start | bytes 1867784 | tf_op jit(solution)/shard_map/ppermute | solution.py:93
  284.1 41.2 %collective-permute-start.7 = (bf16[19,128,128]{2,1,0:T(8,128)(2,1)}, bf16[19,128,128]{2,1,0:T(8,128)(2,1)}, u32[]{:S(2)}, u32[]{:S(2)}) collective-permute-start(bf16[19,128,128]{2,1,0:T(8,128)(2,1)} %get-tuple-element.16), channel_id=1, source_target_pairs={{0,24},{4,28},{8,16},{12,20},{16,8},{20,12},{24,0},{28,4},{1,25},{... | collective-permute-start | bytes 1867784 | tf_op jit(solution)/shard_map/ppermute | solution.py:93
  328.4 19.8 %all-to-all-start.1 = ((bf16[4,19,32,128]{3,2,1,0:T(8,128)(2,1)}), bf16[4,19,32,128]{3,2,1,0:T(8,128)(2,1)S(1)}, u32[]{:S(2)}, u32[]{:S(2)}) async-start(bf16[4,19,32,128]{3,2,1,0:T(8,128)(2,1)} %pad_maximum_fusion.3), calls=%async_computation.1 | async-start | bytes 1245184 | tf_op jit(solution)/shard_map/all_to_all | solution.py:138
  354.0 4.7 %collective-permute-start.8 = (f32[19,1024]{1,0:T(8,128)S(1)}, f32[19,1024]{1,0:T(8,128)S(1)}, u32[]{:S(2)}, u32[]{:S(2)}) collective-permute-start(f32[19,1024]{1,0:T(8,128)S(1)} %fusion.27), channel_id=1, source_target_pairs={{0,1},{1,0},{2,3},{3,2},{4,5},{5,4},{6,7},{7,6},{8,9},{9,8},{10,11... | collective-permute-start | bytes 233480 | tf_op jit(solution)/shard_map/ppermute | solution.py:55
  358.7 6.1 %collective-permute-start.9 = (f32[19,1024]{1,0:T(8,128)S(1)}, f32[19,1024]{1,0:T(8,128)S(1)}, u32[]{:S(2)}, u32[]{:S(2)}) collective-permute-start(f32[19,1024]{1,0:T(8,128)S(1)} %add.327), channel_id=1, source_target_pairs={{0,2},{1,3},{2,0},{3,1},{4,6},{5,7},{6,4},{7,5},{8,10},{9,11},{10,... | collective-permute-start | bytes 233480 | tf_op jit(solution)/shard_map/ppermute | solution.py:55
  (14 other events, 131.8 us)
